TPU v7x, 256 devices: a whole 4x4x8 slice. The times are simulated.
256 devices in a mesh: fsdp: 64 (over x_lo, z, y), dp: 4 (over x_hi, core).
Axes of the slice: x: 4 (x_hi: 2, x_lo: 2; x = x_hi * 2 + x_lo), y: 4, z: 8, core: 2. Of those that a mesh axis runs over, the one named last changes fastest.
Arguments:
- tokens: bfloat16 [4, 8192, 8192], P('dp', 'fsdp'), may hold values from -6 to 6
- queries: bfloat16 [4, 8192, 4096], P('dp', 'fsdp'), may hold values from -40 to 40, as said below
- keys: bfloat16 [4, 8192, 512], P('dp', 'fsdp'), may hold values from -4 to 4
- memory: bfloat16 [4, 8192, 8192], P('dp', 'fsdp'), may hold values from -6 to 6
- mem_keys: bfloat16 [4, 8192, 512], P('dp', 'fsdp'), may hold values from -4 to 4
- cotangent: bfloat16 [4, 8192, 4096], P('dp', 'fsdp'), may hold values from -6 to 6
- value_weight: bfloat16 [8192, 512], P('fsdp'), may hold values from -0.0625 to 0.0625
- dest_group: int32 [4, 128], P('dp', 'fsdp'), may hold values from 0 to 3, as said below
- source_group: int32 [4, 128], P('dp', 'fsdp'), may hold values from 0 to 3, as said below
- lengths: int32 [4, 128], P('dp', 'fsdp'), may hold values from 1 to 64
Outputs:
- grad_queries: bfloat16 [4, 8192, 4096], P('dp', 'fsdp')
- grad_keys: bfloat16 [4, 8192, 512], P('dp', 'fsdp')
- grad_memory: bfloat16 [4, 8192, 8192], P('dp', 'fsdp')
- grad_mem_keys: bfloat16 [4, 8192, 512], P('dp', 'fsdp')
- grad_weight: bfloat16 [8192, 512], P('fsdp')
Inputs may be any that keep to these rules, and one draw needn't show every extreme that they name: `queries`: large in the hidden draw where a query row copies its own key. `dest_group`: the 2 documents of a device go to two different groups, never its own; document k of every device of one fsdp index moves the same number of groups ahead. `source_group`: consistent with dest_group: every device receives exactly one document for each of its slots, at most one from each sender.
All inputs are finite; a program needn't handle non-finite values.
Results may differ from a plain program's by a relative error of at most 0.0075.
Values may be sent and summed in bfloat16 or wider, within the bound.
No kernel may reach another device: no remote copies, remote signals or barrier semaphores. Data moves between devices by JAX's collectives and lax.ppermute only.
A program may use at most 128 MiB of HBM per device.

v0:
```python
import jax
import jax.numpy as jnp
from jax import lax
from jax.sharding import Mesh, PartitionSpec as P

HEAD_DIM = 128


def attend(query_rows, seg_keys, seg_values, slot_keys, slot_values, upstream, length):
    seg_len = query_rows.shape[0]
    mem_len = slot_keys.shape[0]
    kv_width = seg_keys.shape[1]
    heads_kv = kv_width // HEAD_DIM
    group_size = query_rows.shape[1] // kv_width
    key_count = seg_len + mem_len
    all_keys = jnp.concatenate([slot_keys, seg_keys], axis=0).reshape(key_count, heads_kv, HEAD_DIM)
    all_values = jnp.concatenate([slot_values, seg_values], axis=0).reshape(
        key_count, heads_kv, HEAD_DIM
    )
    query_heads = query_rows.reshape(seg_len, heads_kv, group_size, HEAD_DIM)
    score_scale = HEAD_DIM ** (-0.5)
    scores = (
        jnp.einsum("qkgd,jkd->kgqj", query_heads, all_keys, preferred_element_type=jnp.float32)
        * score_scale
    )
    positions = jnp.arange(seg_len)[:, None]
    columns = jnp.arange(key_count)[None, :]
    visible = (columns < mem_len) | (columns - mem_len <= positions)
    scores = jnp.where(visible, scores, -1e30)
    row_max = jnp.max(scores, axis=-1, keepdims=True)
    exp_scores = jnp.exp(scores - row_max)
    weights = exp_scores / jnp.sum(exp_scores, axis=-1, keepdims=True)
    weights_low = weights.astype(jnp.bfloat16)
    output = jnp.einsum(
        "kgqj,jkd->qkgd", weights_low, all_values, preferred_element_type=jnp.float32
    ).astype(jnp.bfloat16)
    live_rows = (jnp.arange(seg_len) < length).astype(jnp.bfloat16)
    masked = (
        upstream.reshape(seg_len, heads_kv, group_size, HEAD_DIM) * live_rows[:, None, None, None]
    )
    grad_weights = jnp.einsum(
        "qkgd,jkd->kgqj", masked, all_values, preferred_element_type=jnp.float32
    )
    grad_values = jnp.einsum(
        "kgqj,qkgd->jkd", weights_low, masked, preferred_element_type=jnp.float32
    ).reshape(key_count, kv_width)
    row_delta = jnp.einsum("qkgd,qkgd->kgq", masked, output, preferred_element_type=jnp.float32)
    grad_scores = (weights * (grad_weights - row_delta[..., None]) * score_scale).astype(
        jnp.bfloat16
    )
    grad_query = (
        jnp.einsum("kgqj,jkd->qkgd", grad_scores, all_keys, preferred_element_type=jnp.float32)
        .reshape(seg_len, -1)
        .astype(jnp.bfloat16)
    )
    grad_all_keys = jnp.einsum(
        "kgqj,qkgd->jkd", grad_scores, query_heads, preferred_element_type=jnp.float32
    ).reshape(key_count, kv_width)
    return (
        grad_query,
        grad_all_keys[:mem_len],
        grad_all_keys[mem_len:],
        grad_values[:mem_len],
        grad_values[mem_len:],
    )


FSDP_AXES = ("fx", "fz", "fy")
DP_AXES = ("dx", "dc")


def to_block_order(cols, split):
    fx, fz, fy = split
    rows = cols.shape[0]
    block = cols.shape[1] // (fx * fz * fy)
    return cols.reshape(rows, fx, fz, fy, block).transpose(0, 2, 3, 1, 4).reshape(rows, -1)


def from_block_order(cols, split):
    fx, fz, fy = split
    rows = cols.shape[0]
    block = cols.shape[1] // (fx * fz * fy)
    return cols.reshape(rows, fz, fy, fx, block).transpose(0, 3, 1, 2, 4).reshape(rows, -1)


def per_device(
    tokens,
    queries,
    keys,
    memory,
    mem_keys,
    cotangent,
    value_weight,
    dest_group,
    source_group,
    lengths,
):
    split = tuple((lax.axis_size(a) for a in FSDP_AXES))
    cores = lax.axis_size("dc")
    groups = lax.axis_size("dx") * cores
    slot_count = dest_group.shape[1]
    seg_len = tokens.shape[1] // slot_count
    mem_len = memory.shape[1] // slot_count
    kv_width = value_weight.shape[1]
    model_width = tokens.shape[2]
    half = kv_width // cores
    core = lax.axis_index("dc")
    part = lax.dynamic_slice_in_dim(value_weight, core * half, half, axis=1)
    part = lax.all_gather(part, "fx", axis=0, tiled=True)
    part = lax.all_gather(part, "fy", axis=0, tiled=True)
    part = lax.all_gather(part, "fz", axis=0, tiled=True)
    weight_full = lax.all_gather(part, "dc", axis=1, tiled=True)
    stacked = to_block_order(jnp.concatenate([tokens[0], memory[0]], axis=0), split)
    partner_stacked = lax.ppermute(stacked, "dc", [(c, (c + 1) % cores) for c in range(cores)])
    values = jnp.dot(stacked, weight_full, preferred_element_type=jnp.float32).astype(jnp.bfloat16)
    split_at = slot_count * seg_len
    seg_values = values[:split_at].reshape(slot_count, seg_len, kv_width)
    doc_values = values[split_at:].reshape(slot_count, mem_len, kv_width)
    doc_keys = mem_keys[0].reshape(slot_count, mem_len, kv_width)
    targets = jnp.arange(groups, dtype=jnp.int32)
    send_table = (dest_group[0][None, :] == targets[:, None]).astype(jnp.bfloat16)
    take_table = (source_group[0][:, None] == targets[None, :]).astype(jnp.bfloat16)
    out_keys = jnp.einsum(
        "hs,smc->hmc", send_table, doc_keys, preferred_element_type=jnp.float32
    ).astype(jnp.bfloat16)
    out_values = jnp.einsum(
        "hs,smc->hmc", send_table, doc_values, preferred_element_type=jnp.float32
    ).astype(jnp.bfloat16)
    in_keys, in_values = (
        lax.all_to_all(out_keys, DP_AXES, split_axis=0, concat_axis=0, tiled=True),
        lax.all_to_all(out_values, DP_AXES, split_axis=0, concat_axis=0, tiled=True),
    )
    slot_keys = jnp.einsum(
        "sh,hmc->smc", take_table, in_keys, preferred_element_type=jnp.float32
    ).astype(jnp.bfloat16)
    slot_values = jnp.einsum(
        "sh,hmc->smc", take_table, in_values, preferred_element_type=jnp.float32
    ).astype(jnp.bfloat16)
    query_slots = queries[0].reshape(slot_count, seg_len, -1)
    key_slots = keys[0].reshape(slot_count, seg_len, kv_width)
    upstream_slots = cotangent[0].reshape(slot_count, seg_len, -1)
    grad_query, slot_grad_keys, seg_grad_keys, slot_grad_values, seg_grad_values = jax.vmap(attend)(
        query_slots, key_slots, seg_values, slot_keys, slot_values, upstream_slots, lengths[0]
    )
    back_keys = jnp.einsum(
        "sh,smc->hmc",
        take_table,
        slot_grad_keys.astype(jnp.bfloat16),
        preferred_element_type=jnp.float32,
    ).astype(jnp.bfloat16)
    back_values = jnp.einsum(
        "sh,smc->hmc",
        take_table,
        slot_grad_values.astype(jnp.bfloat16),
        preferred_element_type=jnp.float32,
    ).astype(jnp.bfloat16)
    ret_keys, ret_values = (
        lax.all_to_all(back_keys, DP_AXES, split_axis=0, concat_axis=0, tiled=True),
        lax.all_to_all(back_values, DP_AXES, split_axis=0, concat_axis=0, tiled=True),
    )
    doc_grad_keys = jnp.einsum(
        "hs,hmc->smc", send_table, ret_keys, preferred_element_type=jnp.float32
    ).astype(jnp.bfloat16)
    doc_grad_values = jnp.einsum(
        "hs,hmc->smc", send_table, ret_values, preferred_element_type=jnp.float32
    ).astype(jnp.bfloat16)
    doc_grad_flat = doc_grad_values.reshape(slot_count * mem_len, kv_width)
    grad_memory = from_block_order(
        lax.dot_general(
            doc_grad_flat, weight_full, (((1,), (1,)), ((), ())), preferred_element_type=jnp.float32
        ).astype(jnp.bfloat16),
        split,
    )
    value_grads_all = jnp.concatenate(
        [seg_grad_values.astype(jnp.bfloat16).reshape(-1, kv_width), doc_grad_flat], axis=0
    )
    grads_half = lax.dynamic_slice_in_dim(value_grads_all, core * half, half, axis=1)
    swap = [(c, (c + 1) % cores) for c in range(cores)]
    partner_grads = lax.ppermute(
        lax.dynamic_slice_in_dim(value_grads_all, (1 - core) * half, half, axis=1), "dc", swap
    )
    both_rows = jnp.concatenate([stacked, partner_stacked], axis=0)
    both_grads = jnp.concatenate([grads_half, partner_grads], axis=0)
    partial = lax.dot_general(
        both_rows, both_grads, (((0,), (0,)), ((), ())), preferred_element_type=jnp.float32
    )
    quarter = half // 2
    fx, fz, fy = split
    first = partial[:, :quarter]
    second = partial[:, quarter:].reshape(fz, fy, fx, -1, quarter).transpose(1, 0, 2, 3, 4)
    second = second.reshape(-1, quarter)
    first = lax.psum_scatter(first, "fz", scatter_dimension=0, tiled=True)
    second = lax.psum_scatter(second, "fy", scatter_dimension=0, tiled=True)
    first = lax.psum_scatter(first, "fy", scatter_dimension=0, tiled=True)
    second = lax.psum_scatter(second, "fz", scatter_dimension=0, tiled=True)
    first = lax.psum_scatter(first, "fx", scatter_dimension=0, tiled=True)
    second = lax.psum_scatter(second, "fx", scatter_dimension=0, tiled=True)
    shares = lax.psum(jnp.concatenate([first, second], axis=1), "dx")
    grad_weight = lax.all_gather(shares, "dc", axis=1, tiled=True).astype(jnp.bfloat16)
    return (
        grad_query.reshape(1, slot_count * seg_len, -1),
        seg_grad_keys.astype(jnp.bfloat16).reshape(1, slot_count * seg_len, kv_width),
        grad_memory.reshape(1, slot_count * mem_len, model_width),
        doc_grad_keys.reshape(1, slot_count * mem_len, kv_width),
        grad_weight,
    )


def refined_mesh(mesh):
    fsdp, dp = (mesh.shape["fsdp"], mesh.shape["dp"])
    devices = mesh.devices.reshape(2, fsdp // 2 // 4, 4, 2, dp // 2)
    return Mesh(devices, FSDP_AXES + DP_AXES)


def solution(mesh):
    fine = refined_mesh(mesh)
    row = P(DP_AXES, FSDP_AXES, None)
    table = P(DP_AXES, FSDP_AXES)
    in_specs = (row, row, row, row, row, row, P(FSDP_AXES, None), table, table, table)
    out_specs = (row, row, row, row, P(FSDP_AXES, None))
    return jax.shard_map(
        per_device, mesh=fine, in_specs=in_specs, out_specs=out_specs, check_vma=False
    )
```

profile of v0, /device:TPU:1, one launch (start us, length us, event | category | flops | bytes accessed | tf_op | source)
XLA Modules:
  0.0 414.3 jit_solution(141352072827042103)
XLA Ops:
  7.2 3.3 copy.65
  10.4 4.1 copy.66
  16.8 2.3 copy.67
  19.0 3.2 collective-permute-start
  23.4 4.0 all-to-all-start
  28.3 5.8 %all-to-all-done = bf16[4,64,512]{2,1,0:T(8,128)(2,1)} async-done(((bf16[4,64,512]{2,1,0:T(8,128)(2,1)}), bf16[4,64,512]{2,1,0:T(8,128)(2,1)}, u32[]{:S(2)}, u32[]{:S(2)}) %all-to-all-start) | async-done | bytes 262176 | tf_op jit(solution)/shard_map/all_to_all | solution.py:130
  42.1 4.3 %all-to-all-start.2 = ((bf16[4,64,512]{2,1,0:T(8,128)(2,1)}), bf16[4,64,512]{2,1,0:T(8,128)(2,1)S(1)}, u32[]{:S(2)}, u32[]{:S(2)}) async-start(bf16[4,64,512]{2,1,0:T(8,128)(2,1)} %copy.78), calls=%async_computation.2 | async-start | bytes 524288 | tf_op jit(solution)/shard_map/all_to_all | solution.py:159
  46.6 6.4 %all-to-all-done.2 = bf16[4,64,512]{2,1,0:T(8,128)(2,1)S(1)} async-done(((bf16[4,64,512]{2,1,0:T(8,128)(2,1)}), bf16[4,64,512]{2,1,0:T(8,128)(2,1)S(1)}, u32[]{:S(2)}, u32[]{:S(2)}) %all-to-all-start.2) | async-done | bytes 262176 | tf_op jit(solution)/shard_map/all_to_all | solution.py:159
  55.5 4.8 %fusion.2 = f32[8192,256]{1,0:T(8,128)S(1)} fusion(bf16[256,8192]{0,1:T(8,128)(2,1)} %collective-permute-done, bf16[256,8192]{0,1:T(8,128)(2,1)} %bitcast.14, bf16[256,256]{1,0:T(8,128)(2,1)S(1)} %collective-permute-done.1, bf16[256,256]{1,0:T(8,128)(2,1)S(1)} %get-tuple-element.7), kind=kOutput, calls=%fused_computation.3 | convolution fusion | flops 2164785152 | bytes 17039360 | tf_op jit(solution)/shard_map/dot_general | solution.py:184
  60.3 3.9 fusion.68
  64.2 4.6 %copy.87 = f32[4,8,2,128,128]{4,3,2,1,0:T(8,128)} copy(f32[4,8,2,128,128]{4,3,2,0,1:T(8,128)} %bitcast.138) | data formatting | bytes 8388608 | tf_op jit(solution)/shard_map/transpose | solution.py:190
  68.9 50.1 %reduce-scatter.7.cloned.1.call-done = f32[1024,128]{1,0:T(8,128)} async-done(((f32[8192,128]{1,0:T(8,128)}), f32[1024,128]{1,0:T(8,128)}) %reduce-scatter.7.cloned.1.call-update) | async-done | bytes 524304 | tf_op jit(solution)/shard_map/reduce_scatter | solution.py:192
  119.1 50.6 %reduce-scatter.13.cloned.1.call-done = f32[2048,128]{1,0:T(8,128)} async-done(((f32[8192,128]{1,0:T(8,128)}), f32[2048,128]{1,0:T(8,128)}) %reduce-scatter.13.cloned.1.call-update) | async-done | bytes 1048592 | tf_op jit(solution)/shard_map/reduce_scatter | solution.py:193
  169.7 3.8 all_gather.15
  173.5 11.0 %all_gather.16 = bf16[1024,256]{1,0:T(8,128)(2,1)} all-gather(bf16[256,256]{1,0:T(8,128)(2,1)S(1)} %all_gather.15), channel_id=1, replica_groups=mesh['fx'=2,'fz'=8,'fy'=4,'dx'=2,'dc'=2] {'fy'}, dimensions={0}, use_global_device_ids=true | all-gather | bytes 655360 | tf_op jit(solution)/shard_map/all_gather | solution.py:110
  184.6 9.3 %reduce-scatter.9.cloned.1.call-done = f32[256,128]{1,0:T(8,128)} async-done(((f32[1024,128]{1,0:T(8,128)}), f32[256,128]{1,0:T(8,128)}) %reduce-scatter.9.cloned.1.call-update) | async-done | bytes 131088 | tf_op jit(solution)/shard_map/reduce_scatter | solution.py:194
  193.9 38.3 %reduce-scatter.15.cloned.1.call-done = f32[256,128]{1,0:T(8,128)} async-done(((f32[2048,128]{1,0:T(8,128)}), f32[256,128]{1,0:T(8,128)}) %reduce-scatter.15.cloned.1.call-update) | async-done | bytes 131088 | tf_op jit(solution)/shard_map/reduce_scatter | solution.py:195
  232.3 59.8 %all-gather.3.cloned.1.call-done = bf16[8192,256]{1,0:T(8,128)(2,1)} async-done(((bf16[1024,256]{1,0:T(8,128)(2,1)}), bf16[8192,256]{1,0:T(8,128)(2,1)}) %all-gather.3.cloned.1.call-update) | async-done | bytes 4194320 | tf_op jit(solution)/shard_map/all_gather | solution.py:111
  292.2 16.3 %reduce-scatter.11.cloned.1.call-done = f32[128,128]{1,0:T(8,128)} async-done(((f32[256,128]{1,0:T(8,128)}), f32[128,128]{1,0:T(8,128)}) %reduce-scatter.11.cloned.1.call-update) | async-done | bytes 65552 | tf_op jit(solution)/shard_map/reduce_scatter | solution.py:196
  308.5 18.9 %reduce-scatter.17.cloned.1.call-done = f32[128,128]{1,0:T(8,128)} async-done(((f32[256,128]{1,0:T(8,128)}), f32[128,128]{1,0:T(8,128)}) %reduce-scatter.17.cloned.1.call-update) | async-done | bytes 65552 | tf_op jit(solution)/shard_map/reduce_scatter | solution.py:197
  328.3 10.4 %all-reduce.1 = bf16[128,256]{1,0:T(8,128)(2,1)S(1)} all-reduce(f32[128,256]{1,0:T(8,128)S(1)} %pad_maximum_fusion), channel_id=1, replica_groups=mesh['fx'=2,'fz'=8,'fy'=4,'dx'=2,'dc'=2] {'dx'}, use_global_device_ids=true, to_apply=%region_8.9 | all-reduce | flops 32768 | bytes 196608 | tf_op jit(solution)/shard_map/psum | solution.py:198
  338.7 4.8 %all_gather.19 = bf16[128,512]{1,0:T(8,128)(2,1)} all-gather(bf16[128,256]{1,0:T(8,128)(2,1)S(1)} %all-reduce.1), channel_id=1, replica_groups=mesh['fx'=2,'fz'=8,'fy'=4,'dx'=2,'dc'=2] {'dc'}, dimensions={1}, use_global_device_ids=true | all-gather | bytes 196608 | tf_op jit(solution)/shard_map/all_gather | solution.py:199
  343.5 11.1 %all-gather.5.cloned.1.call-done = bf16[8192,512]{1,0:T(8,128)(2,1)} async-done(((bf16[8192,256]{1,0:T(8,128)(2,1)}), bf16[8192,512]{1,0:T(8,128)(2,1)}) %all-gather.5.cloned.1.call-update) | async-done | bytes 8388624 | tf_op jit(solution)/shard_map/all_gather | solution.py:112
  354.6 7.0 %convolution_convert_fusion.7 = bf16[256,512]{1,0:T(8,128)(2,1)S(1)} fusion(bf16[256,8192]{0,1:T(8,128)(2,1)} %bitcast.14, bf16[8192,512]{1,0:T(8,128)(2,1)} %all-gather.5.cloned.1.call-done), kind=kOutput, calls=%fused_computation.29 | convolution fusion | flops 2147614720 | bytes 12845056 | tf_op jit(solution)/shard_map/dot_general | solution.py:115
  362.8 4.2 %all-to-all-start.1 = ((bf16[4,64,512]{2,1,0:T(8,128)(2,1)}), bf16[4,64,512]{2,1,0:T(8,128)(2,1)}, u32[]{:S(2)}, u32[]{:S(2)}) async-start(bf16[4,64,512]{2,1,0:T(8,128)(2,1)} %copy.69), calls=%async_computation.1 | async-start | bytes 524288 | tf_op jit(solution)/shard_map/all_to_all | solution.py:131
  367.0 7.5 %convolution_convert_fusion = bf16[128,8192]{1,0:T(8,128)(2,1)} fusion(bf16[128,512]{1,0:T(8,128)(2,1)S(1)} %bitcast.146, bf16[8192,512]{1,0:T(8,128)(2,1)} %all-gather.5.cloned.1.call-done), kind=kOutput, calls=%fused_computation.2 | convolution fusion | flops 1074790400 | bytes 10616832 | tf_op jit(solution)/shard_map/dot_general | solution.py:169
  374.6 3.2 reshape.115
  377.9 2.5 copy.81
  380.4 4.6 %reshape_reshape.3 = bf16[1,128,8192]{2,1,0:T(8,128)(2,1)} reshape(bf16[128,2,8,4,128]{4,3,2,1,0:T(4,128)(2,1)} %copy.81) | data formatting | bytes 4194304 | tf_op jit(solution)/shard_map/reshape;reshape | solution.py:203
  389.3 2.9 fusion.8
  394.4 4.8 %all-to-all-start.3 = ((bf16[4,64,512]{2,1,0:T(8,128)(2,1)}), bf16[4,64,512]{2,1,0:T(8,128)(2,1)S(1)}, u32[]{:S(2)}, u32[]{:S(2)}) async-start(bf16[4,64,512]{2,1,0:T(8,128)(2,1)} %copy.83), calls=%async_computation.3 | async-start | bytes 524288 | tf_op jit(solution)/shard_map/all_to_all | solution.py:158
  402.5 3.3 all-to-all-done.3
  (100 shorter events, 28.6 us)
Async XLA Ops:
  7.2 15.1 %copy-start = (bf16[1,128,512]{2,1,0:T(8,128)(2,1)S(1)}, bf16[1,128,512]{2,1,0:T(8,128)(2,1)}, u32[]{:S(2)}) copy-start(bf16[1,128,512]{2,1,0:T(8,128)(2,1)} %param.14) | copy-start | bytes 393220
  16.7 5.5 %copy-start.15 = (s32[1,2]{1,0:T(1,128)S(1)}, s32[1,2]{1,0:T(1,128)}, u32[]{:S(2)}) copy-start(s32[1,2]{1,0:T(1,128)} %param.17) | copy-start | bytes 28
  16.8 10.7 %copy-start.10 = (bf16[1,128,512]{2,1,0:T(8,128)(2,1)S(1)}, bf16[1,128,512]{2,1,0:T(8,128)(2,1)}, u32[]{:S(2)}) copy-start(bf16[1,128,512]{2,1,0:T(8,128)(2,1)} %param.12) | copy-start | bytes 393220
  19.0 8.5 %copy-start.4 = (bf16[1,128,4096]{2,1,0:T(8,128)(2,1)S(1)}, bf16[1,128,4096]{2,1,0:T(8,128)(2,1)}, u32[]{:S(2)}) copy-start(bf16[1,128,4096]{2,1,0:T(8,128)(2,1)} %param.11) | copy-start | bytes 3145732
  19.0 36.5 %collective-permute-start = (bf16[256,8192]{0,1:T(8,128)(2,1)}, bf16[256,8192]{0,1:T(8,128)(2,1)}, u32[]{:S(2)}, u32[]{:S(2)}) collective-permute-start(bf16[256,8192]{0,1:T(8,128)(2,1)} %bitcast.14), channel_id=1, source_target_pairs={{0,1},{1,0},{2,3},{3,2},{4,5},{5,4},{6,7},{7,6},{8,9},{9,8},{10,11... | collective-permute-start | bytes 12582920 | tf_op jit(solution)/shard_map/ppermute | solution.py:114
  22.2 5.6 %copy-start.5 = (bf16[1,128,4096]{2,1,0:T(8,128)(2,1)S(1)}, bf16[1,128,4096]{2,1,0:T(8,128)(2,1)}, u32[]{:S(2)}) copy-start(bf16[1,128,4096]{2,1,0:T(8,128)(2,1)} %param.15) | copy-start | bytes 3145732
  23.4 10.7 %all-to-all-start = ((bf16[4,64,512]{2,1,0:T(8,128)(2,1)}), bf16[4,64,512]{2,1,0:T(8,128)(2,1)}, u32[]{:S(2)}, u32[]{:S(2)}) async-start(bf16[4,64,512]{2,1,0:T(8,128)(2,1)} %copy.60), calls=%async_computation | async-start | bytes 524288 | tf_op jit(solution)/shard_map/all_to_all | solution.py:130
  27.5 0.7 copy-start.13
  27.5 6.5 %copy-start.14 = (s32[1,2]{1,0:T(1,128)S(1)}, s32[1,2]{1,0:T(1,128)}, u32[]{:S(2)}) copy-start(s32[1,2]{1,0:T(1,128)} %param.18) | copy-start | bytes 28
  27.8 9.9 %copy-start.6 = (bf16[16,8,32,128]{3,2,1,0:T(8,128)(2,1)}, bf16[16,8,32,128]{3,2,1,0:T(8,128)(2,1)S(1)}, u32[]{:S(2)}) copy-start(bf16[16,8,32,128]{3,2,1,0:T(8,128)(2,1)S(1)} %copy.102) | copy-start | bytes 3145732
  28.1 11.6 %copy-start.2 = (bf16[16,8,32,128]{3,2,1,0:T(8,128)(2,1)}, bf16[16,8,32,128]{3,2,1,0:T(8,128)(2,1)S(1)}, u32[]{:S(2)}) copy-start(bf16[16,8,32,128]{3,2,1,0:T(8,128)(2,1)S(1)} %copy.103) | copy-start | bytes 3145732
  37.8 2.9 copy-start.11
  42.1 10.9 %all-to-all-start.2 = ((bf16[4,64,512]{2,1,0:T(8,128)(2,1)}), bf16[4,64,512]{2,1,0:T(8,128)(2,1)S(1)}, u32[]{:S(2)}, u32[]{:S(2)}) async-start(bf16[4,64,512]{2,1,0:T(8,128)(2,1)} %copy.78), calls=%async_computation.2 | async-start | bytes 524288 | tf_op jit(solution)/shard_map/all_to_all | solution.py:159
  46.5 72.6 %reduce-scatter.7.cloned.1.call-start = ((), (), s32[]{:S(2)}) async-start(), calls=%async_computation.12 | async-start | bytes 4718592 | tf_op jit(solution)/shard_map/reduce_scatter | solution.py:192
  53.4 2.0 collective-permute-start.1
  64.2 105.5 %reduce-scatter.13.cloned.1.call-start = ((), (), s32[]{:S(2)}) async-start(), calls=%async_computation.15 | async-start | bytes 5242880 | tf_op jit(solution)/shard_map/reduce_scatter | solution.py:193
  68.9 100.9 %copy-start.12 = (bf16[128,512]{1,0:T(8,128)(2,1)S(1)}, bf16[128,512]{1,0:T(8,128)(2,1)}, u32[]{:S(2)}) copy-start(bf16[128,512]{1,0:T(8,128)(2,1)} %param.16) | copy-start | bytes 393220
  68.9 125.0 %reduce-scatter.9.cloned.1.call-start = ((), (), s32[]{:S(2)}) async-start(), calls=%async_computation.13 | async-start | bytes 655360 | tf_op jit(solution)/shard_map/reduce_scatter | solution.py:194
  119.0 113.2 %reduce-scatter.15.cloned.1.call-start = ((), (), s32[]{:S(2)}) async-start(), calls=%async_computation.16 | async-start | bytes 1179648 | tf_op jit(solution)/shard_map/reduce_scatter | solution.py:195
  169.7 122.5 %all-gather.3.cloned.1.call-start = ((), (), s32[]{:S(2)}) async-start(), calls=%async_computation.10 | async-start | bytes 4718592 | tf_op jit(solution)/shard_map/all_gather | solution.py:111
  184.5 123.9 %reduce-scatter.11.cloned.1.call-start = ((), (), s32[]{:S(2)}) async-start(), calls=%async_computation.14 | async-start | bytes 196608 | tf_op jit(solution)/shard_map/reduce_scatter | solution.py:196
  193.9 133.5 %reduce-scatter.17.cloned.1.call-start = ((), (), s32[]{:S(2)}) async-start(), calls=%async_computation.17 | async-start | bytes 196608 | tf_op jit(solution)/shard_map/reduce_scatter | solution.py:197
  232.3 122.3 %all-gather.5.cloned.1.call-start = ((), (), s32[]{:S(2)}) async-start(), calls=%async_computation.11 | async-start | bytes 12582912 | tf_op jit(solution)/shard_map/all_gather | solution.py:112
  362.8 22.2 %all-to-all-start.1 = ((bf16[4,64,512]{2,1,0:T(8,128)(2,1)}), bf16[4,64,512]{2,1,0:T(8,128)(2,1)}, u32[]{:S(2)}, u32[]{:S(2)}) async-start(bf16[4,64,512]{2,1,0:T(8,128)(2,1)} %copy.69), calls=%async_computation.1 | async-start | bytes 524288 | tf_op jit(solution)/shard_map/all_to_all | solution.py:131
  380.4 6.7 %copy-start.3 = (bf16[16,8,32,128]{3,2,1,0:T(8,128)(2,1)S(1)}, bf16[16,8,32,128]{3,2,1,0:T(8,128)(2,1)}, u32[]{:S(2)}) copy-start(bf16[16,8,32,128]{3,2,1,0:T(8,128)(2,1)} %copy-done.2) | copy-start | bytes 3145732
  386.4 0.7 copy-start.8
  389.3 2.9 copy-start.7
  394.4 11.3 %all-to-all-start.3 = ((bf16[4,64,512]{2,1,0:T(8,128)(2,1)}), bf16[4,64,512]{2,1,0:T(8,128)(2,1)S(1)}, u32[]{:S(2)}, u32[]{:S(2)}) async-start(bf16[4,64,512]{2,1,0:T(8,128)(2,1)} %copy.83), calls=%async_computation.3 | async-start | bytes 524288 | tf_op jit(solution)/shard_map/all_to_all | solution.py:158
  399.7 7.8 %copy-start.1 = (bf16[1,128,512]{2,1,0:T(8,128)(2,1)S(1)}, bf16[1,128,512]{2,1,0:T(8,128)(2,1)}, u32[]{:S(2)}) copy-start(bf16[1,128,512]{2,1,0:T(8,128)(2,1)} %param.14) | copy-start | bytes 393220
  400.4 6.4 %copy-start.9 = (bf16[128,512]{1,0:T(8,128)(2,1)S(1)}, bf16[128,512]{1,0:T(8,128)(2,1)}, u32[]{:S(2)}) copy-start(bf16[128,512]{1,0:T(8,128)(2,1)} %all_gather.19) | copy-start | bytes 393220
Sparse Core Ops, SparseCore 0:
  64.3 54.6 reduce-scatter.6
  121.6 48.0 reduce-scatter.12
  172.2 21.6 reduce-scatter.8
  196.3 35.9 reduce-scatter.14
  233.9 58.2 all-gather.2
  294.5 13.9 reduce-scatter.10
  310.9 16.4 reduce-scatter.16
  329.2 25.3 all-gather.4
where the time goes:
time: 415 us; the launch traced here: 414 us
  waiting for transfers between devices  271 us (65%)
  local copies, waits for them, and re-layouts  37.9 us (9%)
  matrix products  33.7 us (8%)
  blocking collectives  29.9 us (7%)
  starting transfers between devices  22 us (5%)
  between operations  14.6 us (4%)
  other arithmetic  5.17 us (1%)
    all_gather x1, waiting for transfers between devices, per_device(): part = lax.all_gather(part, 'fz', axis=0, tiled=True)  59.8 us
    reduce_scatter x1, waiting for transfers between devices, per_device(): second = lax.psum_scatter(second, 'fy', scatter_dimension=0, tiled=True)  50.6 us
    reduce_scatter x1, waiting for transfers between devices, per_device(): first = lax.psum_scatter(first, 'fz', scatter_dimension=0, tiled=True)  50.1 us
    reduce_scatter x1, waiting for transfers between devices, per_device(): second = lax.psum_scatter(second, 'fz', scatter_dimension=0, tiled=True)  38.3 us
    reduce_scatter x1, waiting for transfers between devices, per_device(): second = lax.psum_scatter(second, 'fx', scatter_dimension=0, tiled=True)  18.9 us
    reduce_scatter x1, waiting for transfers between devices, per_device(): first = lax.psum_scatter(first, 'fx', scatter_dimension=0, tiled=True)  16.3 us
    all_gather x1, waiting for transfers between devices, per_device(): weight_full = lax.all_gather(part, 'dc', axis=1, tiled=True)  11.1 us
    all_gather x1, blocking collectives, per_device(): part = lax.all_gather(part, 'fy', axis=0, tiled=True)  11 us
  transfers between devices with their start and end apart: 14, of which 12 were waited for; matrix products, arithmetic and copies ran while one was open for 9% of the time, Pallas kernels for 0%

commit v1 on v0

--- a/solution.py
+++ b/solution.py
@@ -195,7 +195,7 @@
     second = lax.psum_scatter(second, "fz", scatter_dimension=0, tiled=True)
     first = lax.psum_scatter(first, "fx", scatter_dimension=0, tiled=True)
     second = lax.psum_scatter(second, "fx", scatter_dimension=0, tiled=True)
-    shares = lax.psum(jnp.concatenate([first, second], axis=1), "dx")
+    shares = jnp.sum(lax.all_gather(jnp.concatenate([first, second], axis=1), "dx"), axis=0)
     grad_weight = lax.all_gather(shares, "dc", axis=1, tiled=True).astype(jnp.bfloat16)
     return (
         grad_query.reshape(1, slot_count * seg_len, -1),

time: 415 us -> 415 us (level)
  blocking collectives: 29.9 us -> 24.7 us
  waiting for transfers between devices: 271 us -> 276 us
    psum x1 -> x0, blocking collectives: 10.4 us -> none  [per_device(): shares = lax.psum(jnp.concatenate([first, second], axis=1), 'dx')]
    all_gather x0 -> x1, blocking collectives: none -> 6.32 us  [per_device(): lax.all_gather(jnp.concatenate([first, second], axis=1), 'dx')]
    all_gather x1, waiting for transfers between devices: 11.1 us -> 16.3 us  [per_device(): weight_full = lax.all_gather(part, 'dc', axis=1, tiled=True)]
where the time goes in v1:
time: 415 us; the launch traced here: 414 us
  waiting for transfers between devices  276 us (67%)
  local copies, waits for them, and re-layouts  37.9 us (9%)
  matrix products  33.7 us (8%)
  blocking collectives  24.7 us (6%)
  starting transfers between devices  22 us (5%)
  between operations  14.6 us (4%)
  other arithmetic  5.19 us (1%)
    all_gather x1, waiting for transfers between devices, per_device(): part = lax.all_gather(part, 'fz', axis=0, tiled=True)  59.8 us
    reduce_scatter x1, waiting for transfers between devices, per_device(): second = lax.psum_scatter(second, 'fy', scatter_dimension=0, tiled=True)  50.6 us
    reduce_scatter x1, waiting for transfers between devices, per_device(): first = lax.psum_scatter(first, 'fz', scatter_dimension=0, tiled=True)  50.1 us
    reduce_scatter x1, waiting for transfers between devices, per_device(): second = lax.psum_scatter(second, 'fz', scatter_dimension=0, tiled=True)  38.3 us
    reduce_scatter x1, waiting for transfers between devices, per_device(): second = lax.psum_scatter(second, 'fx', scatter_dimension=0, tiled=True)  18.9 us
    all_gather x1, waiting for transfers between devices, per_device(): weight_full = lax.all_gather(part, 'dc', axis=1, tiled=True)  16.3 us
    reduce_scatter x1, waiting for transfers between devices, per_device(): first = lax.psum_scatter(first, 'fx', scatter_dimension=0, tiled=True)  16.3 us
    all_gather x1, blocking collectives, per_device(): part = lax.all_gather(part, 'fy', axis=0, tiled=True)  11 us
  transfers between devices with their start and end apart: 14, of which 12 were waited for; matrix products, arithmetic and copies ran while one was open for 9% of the time, Pallas kernels for 0%

profile of v1, /device:TPU:1, one launch (start us, length us, event | category | flops | bytes accessed | tf_op | source)
XLA Modules:
  0.0 414.3 jit_solution(3784056949232613589)
XLA Ops:
  7.2 3.3 copy.65
  10.4 4.1 copy.66
  16.8 2.3 copy.67
  19.0 3.2 collective-permute-start
  23.4 4.0 all-to-all-start
  28.3 5.8 %all-to-all-done = bf16[4,64,512]{2,1,0:T(8,128)(2,1)} async-done(((bf16[4,64,512]{2,1,0:T(8,128)(2,1)}), bf16[4,64,512]{2,1,0:T(8,128)(2,1)}, u32[]{:S(2)}, u32[]{:S(2)}) %all-to-all-start) | async-done | bytes 262176 | tf_op jit(solution)/shard_map/all_to_all | solution.py:130
  42.1 4.3 %all-to-all-start.2 = ((bf16[4,64,512]{2,1,0:T(8,128)(2,1)}), bf16[4,64,512]{2,1,0:T(8,128)(2,1)S(1)}, u32[]{:S(2)}, u32[]{:S(2)}) async-start(bf16[4,64,512]{2,1,0:T(8,128)(2,1)} %copy.78), calls=%async_computation.2 | async-start | bytes 524288 | tf_op jit(solution)/shard_map/all_to_all | solution.py:159
  46.6 6.4 %all-to-all-done.2 = bf16[4,64,512]{2,1,0:T(8,128)(2,1)S(1)} async-done(((bf16[4,64,512]{2,1,0:T(8,128)(2,1)}), bf16[4,64,512]{2,1,0:T(8,128)(2,1)S(1)}, u32[]{:S(2)}, u32[]{:S(2)}) %all-to-all-start.2) | async-done | bytes 262176 | tf_op jit(solution)/shard_map/all_to_all | solution.py:159
  55.5 4.8 %fusion.2 = f32[8192,256]{1,0:T(8,128)S(1)} fusion(bf16[256,8192]{0,1:T(8,128)(2,1)} %collective-permute-done, bf16[256,8192]{0,1:T(8,128)(2,1)} %bitcast.14, bf16[256,256]{1,0:T(8,128)(2,1)S(1)} %collective-permute-done.1, bf16[256,256]{1,0:T(8,128)(2,1)S(1)} %get-tuple-element.7), kind=kOutput, calls=%fused_computation.3 | convolution fusion | flops 2164785152 | bytes 17039360 | tf_op jit(solution)/shard_map/dot_general | solution.py:184
  60.3 3.9 fusion.68
  64.2 4.6 %copy.87 = f32[4,8,2,128,128]{4,3,2,1,0:T(8,128)} copy(f32[4,8,2,128,128]{4,3,2,0,1:T(8,128)} %bitcast.139) | data formatting | bytes 8388608 | tf_op jit(solution)/shard_map/transpose | solution.py:190
  68.9 50.1 %reduce-scatter.7.cloned.1.call-done = f32[1024,128]{1,0:T(8,128)} async-done(((f32[8192,128]{1,0:T(8,128)}), f32[1024,128]{1,0:T(8,128)}) %reduce-scatter.7.cloned.1.call-update) | async-done | bytes 524304 | tf_op jit(solution)/shard_map/reduce_scatter | solution.py:192
  119.1 50.6 %reduce-scatter.13.cloned.1.call-done = f32[2048,128]{1,0:T(8,128)} async-done(((f32[8192,128]{1,0:T(8,128)}), f32[2048,128]{1,0:T(8,128)}) %reduce-scatter.13.cloned.1.call-update) | async-done | bytes 1048592 | tf_op jit(solution)/shard_map/reduce_scatter | solution.py:193
  169.7 3.8 all_gather.21
  173.5 11.0 %all_gather.22 = bf16[1024,256]{1,0:T(8,128)(2,1)} all-gather(bf16[256,256]{1,0:T(8,128)(2,1)S(1)} %all_gather.21), channel_id=1, replica_groups=mesh['fx'=2,'fz'=8,'fy'=4,'dx'=2,'dc'=2] {'fy'}, dimensions={0}, use_global_device_ids=true | all-gather | bytes 655360 | tf_op jit(solution)/shard_map/all_gather | solution.py:110
  184.6 9.3 %reduce-scatter.9.cloned.1.call-done = f32[256,128]{1,0:T(8,128)} async-done(((f32[1024,128]{1,0:T(8,128)}), f32[256,128]{1,0:T(8,128)}) %reduce-scatter.9.cloned.1.call-update) | async-done | bytes 131088 | tf_op jit(solution)/shard_map/reduce_scatter | solution.py:194
  193.9 38.3 %reduce-scatter.15.cloned.1.call-done = f32[256,128]{1,0:T(8,128)} async-done(((f32[2048,128]{1,0:T(8,128)}), f32[256,128]{1,0:T(8,128)}) %reduce-scatter.15.cloned.1.call-update) | async-done | bytes 131088 | tf_op jit(solution)/shard_map/reduce_scatter | solution.py:195
  232.3 59.8 %all-gather.4.cloned.1.call-done = bf16[8192,256]{1,0:T(8,128)(2,1)} async-done(((bf16[1024,256]{1,0:T(8,128)(2,1)}), bf16[8192,256]{1,0:T(8,128)(2,1)}) %all-gather.4.cloned.1.call-update) | async-done | bytes 4194320 | tf_op jit(solution)/shard_map/all_gather | solution.py:111
  292.2 16.3 %reduce-scatter.11.cloned.1.call-done = f32[128,128]{1,0:T(8,128)} async-done(((f32[256,128]{1,0:T(8,128)}), f32[128,128]{1,0:T(8,128)}) %reduce-scatter.11.cloned.1.call-update) | async-done | bytes 65552 | tf_op jit(solution)/shard_map/reduce_scatter | solution.py:196
  308.5 18.9 %reduce-scatter.17.cloned.1.call-done = f32[128,128]{1,0:T(8,128)} async-done(((f32[256,128]{1,0:T(8,128)}), f32[128,128]{1,0:T(8,128)}) %reduce-scatter.17.cloned.1.call-update) | async-done | bytes 65552 | tf_op jit(solution)/shard_map/reduce_scatter | solution.py:197
  328.3 6.3 %all-gather = f32[256,256]{1,0:T(8,128)S(1)} all-gather(f32[128,256]{1,0:T(8,128)S(1)} %pad_maximum_fusion), channel_id=2, replica_groups=mesh['fx'=2,'fz'=8,'fy'=4,'dx'=2,'dc'=2] {'dx'}, dimensions={0}, use_global_device_ids=true | all-gather | bytes 393216 | tf_op jit(solution)/shard_map/all_gather | solution.py:198
  334.6 3.6 all_gather.27
  338.2 16.3 %all-gather.6.cloned.1.call-done = bf16[8192,512]{1,0:T(8,128)(2,1)} async-done(((bf16[8192,256]{1,0:T(8,128)(2,1)}), bf16[8192,512]{1,0:T(8,128)(2,1)}) %all-gather.6.cloned.1.call-update) | async-done | bytes 8388624 | tf_op jit(solution)/shard_map/all_gather | solution.py:112
  354.6 7.0 %convolution_convert_fusion.7 = bf16[256,512]{1,0:T(8,128)(2,1)S(1)} fusion(bf16[256,8192]{0,1:T(8,128)(2,1)} %bitcast.14, bf16[8192,512]{1,0:T(8,128)(2,1)} %all-gather.6.cloned.1.call-done), kind=kOutput, calls=%fused_computation.29 | convolution fusion | flops 2147614720 | bytes 12845056 | tf_op jit(solution)/shard_map/dot_general | solution.py:115
  362.8 4.2 %all-to-all-start.1 = ((bf16[4,64,512]{2,1,0:T(8,128)(2,1)}), bf16[4,64,512]{2,1,0:T(8,128)(2,1)}, u32[]{:S(2)}, u32[]{:S(2)}) async-start(bf16[4,64,512]{2,1,0:T(8,128)(2,1)} %copy.69), calls=%async_computation.1 | async-start | bytes 524288 | tf_op jit(solution)/shard_map/all_to_all | solution.py:131
  367.0 7.5 %convolution_convert_fusion = bf16[128,8192]{1,0:T(8,128)(2,1)} fusion(bf16[128,512]{1,0:T(8,128)(2,1)S(1)} %bitcast.147, bf16[8192,512]{1,0:T(8,128)(2,1)} %all-gather.6.cloned.1.call-done), kind=kOutput, calls=%fused_computation.2 | convolution fusion | flops 1074790400 | bytes 10616832 | tf_op jit(solution)/shard_map/dot_general | solution.py:169
  374.6 3.2 reshape.115
  377.9 2.5 copy.81
  380.4 4.6 %reshape_reshape.3 = bf16[1,128,8192]{2,1,0:T(8,128)(2,1)} reshape(bf16[128,2,8,4,128]{4,3,2,1,0:T(4,128)(2,1)} %copy.81) | data formatting | bytes 4194304 | tf_op jit(solution)/shard_map/reshape;reshape | solution.py:203
  389.3 2.9 fusion.8
  394.4 4.8 %all-to-all-start.3 = ((bf16[4,64,512]{2,1,0:T(8,128)(2,1)}), bf16[4,64,512]{2,1,0:T(8,128)(2,1)S(1)}, u32[]{:S(2)}, u32[]{:S(2)}) async-start(bf16[4,64,512]{2,1,0:T(8,128)(2,1)} %copy.83), calls=%async_computation.3 | async-start | bytes 524288 | tf_op jit(solution)/shard_map/all_to_all | solution.py:158
  402.5 3.3 all-to-all-done.3
  (101 shorter events, 28.6 us)
Async XLA Ops:
  7.2 15.1 %copy-start = (bf16[1,128,512]{2,1,0:T(8,128)(2,1)S(1)}, bf16[1,128,512]{2,1,0:T(8,128)(2,1)}, u32[]{:S(2)}) copy-start(bf16[1,128,512]{2,1,0:T(8,128)(2,1)} %param.14) | copy-start | bytes 393220
  16.7 5.5 %copy-start.15 = (s32[1,2]{1,0:T(1,128)S(1)}, s32[1,2]{1,0:T(1,128)}, u32[]{:S(2)}) copy-start(s32[1,2]{1,0:T(1,128)} %param.17) | copy-start | bytes 28
  16.8 10.7 %copy-start.10 = (bf16[1,128,512]{2,1,0:T(8,128)(2,1)S(1)}, bf16[1,128,512]{2,1,0:T(8,128)(2,1)}, u32[]{:S(2)}) copy-start(bf16[1,128,512]{2,1,0:T(8,128)(2,1)} %param.12) | copy-start | bytes 393220
  19.0 8.5 %copy-start.4 = (bf16[1,128,4096]{2,1,0:T(8,128)(2,1)S(1)}, bf16[1,128,4096]{2,1,0:T(8,128)(2,1)}, u32[]{:S(2)}) copy-start(bf16[1,128,4096]{2,1,0:T(8,128)(2,1)} %param.11) | copy-start | bytes 3145732
  19.0 36.5 %collective-permute-start = (bf16[256,8192]{0,1:T(8,128)(2,1)}, bf16[256,8192]{0,1:T(8,128)(2,1)}, u32[]{:S(2)}, u32[]{:S(2)}) collective-permute-start(bf16[256,8192]{0,1:T(8,128)(2,1)} %bitcast.14), channel_id=1, source_target_pairs={{0,1},{1,0},{2,3},{3,2},{4,5},{5,4},{6,7},{7,6},{8,9},{9,8},{10,11... | collective-permute-start | bytes 12582920 | tf_op jit(solution)/shard_map/ppermute | solution.py:114
  22.2 5.6 %copy-start.5 = (bf16[1,128,4096]{2,1,0:T(8,128)(2,1)S(1)}, bf16[1,128,4096]{2,1,0:T(8,128)(2,1)}, u32[]{:S(2)}) copy-start(bf16[1,128,4096]{2,1,0:T(8,128)(2,1)} %param.15) | copy-start | bytes 3145732
  23.4 10.7 %all-to-all-start = ((bf16[4,64,512]{2,1,0:T(8,128)(2,1)}), bf16[4,64,512]{2,1,0:T(8,128)(2,1)}, u32[]{:S(2)}, u32[]{:S(2)}) async-start(bf16[4,64,512]{2,1,0:T(8,128)(2,1)} %copy.60), calls=%async_computation | async-start | bytes 524288 | tf_op jit(solution)/shard_map/all_to_all | solution.py:130
  27.5 0.7 copy-start.13
  27.5 6.5 %copy-start.14 = (s32[1,2]{1,0:T(1,128)S(1)}, s32[1,2]{1,0:T(1,128)}, u32[]{:S(2)}) copy-start(s32[1,2]{1,0:T(1,128)} %param.18) | copy-start | bytes 28
  27.8 9.9 %copy-start.6 = (bf16[16,8,32,128]{3,2,1,0:T(8,128)(2,1)}, bf16[16,8,32,128]{3,2,1,0:T(8,128)(2,1)S(1)}, u32[]{:S(2)}) copy-start(bf16[16,8,32,128]{3,2,1,0:T(8,128)(2,1)S(1)} %copy.102) | copy-start | bytes 3145732
  28.1 11.6 %copy-start.2 = (bf16[16,8,32,128]{3,2,1,0:T(8,128)(2,1)}, bf16[16,8,32,128]{3,2,1,0:T(8,128)(2,1)S(1)}, u32[]{:S(2)}) copy-start(bf16[16,8,32,128]{3,2,1,0:T(8,128)(2,1)S(1)} %copy.103) | copy-start | bytes 3145732
  37.8 2.9 copy-start.11
  42.1 10.9 %all-to-all-start.2 = ((bf16[4,64,512]{2,1,0:T(8,128)(2,1)}), bf16[4,64,512]{2,1,0:T(8,128)(2,1)S(1)}, u32[]{:S(2)}, u32[]{:S(2)}) async-start(bf16[4,64,512]{2,1,0:T(8,128)(2,1)} %copy.78), calls=%async_computation.2 | async-start | bytes 524288 | tf_op jit(solution)/shard_map/all_to_all | solution.py:159
  46.5 72.6 %reduce-scatter.7.cloned.1.call-start = ((), (), s32[]{:S(2)}) async-start(), calls=%async_computation.12 | async-start | bytes 4718592 | tf_op jit(solution)/shard_map/reduce_scatter | solution.py:192
  53.4 2.0 collective-permute-start.1
  64.2 105.5 %reduce-scatter.13.cloned.1.call-start = ((), (), s32[]{:S(2)}) async-start(), calls=%async_computation.15 | async-start | bytes 5242880 | tf_op jit(solution)/shard_map/reduce_scatter | solution.py:193
  68.9 100.9 %copy-start.12 = (bf16[128,512]{1,0:T(8,128)(2,1)S(1)}, bf16[128,512]{1,0:T(8,128)(2,1)}, u32[]{:S(2)}) copy-start(bf16[128,512]{1,0:T(8,128)(2,1)} %param.16) | copy-start | bytes 393220
  68.9 125.0 %reduce-scatter.9.cloned.1.call-start = ((), (), s32[]{:S(2)}) async-start(), calls=%async_computation.13 | async-start | bytes 655360 | tf_op jit(solution)/shard_map/reduce_scatter | solution.py:194
  119.0 113.2 %reduce-scatter.15.cloned.1.call-start = ((), (), s32[]{:S(2)}) async-start(), calls=%async_computation.16 | async-start | bytes 1179648 | tf_op jit(solution)/shard_map/reduce_scatter | solution.py:195
  169.7 122.5 %all-gather.4.cloned.1.call-start = ((), (), s32[]{:S(2)}) async-start(), calls=%async_computation.10 | async-start | bytes 4718592 | tf_op jit(solution)/shard_map/all_gather | solution.py:111
  184.5 123.9 %reduce-scatter.11.cloned.1.call-start = ((), (), s32[]{:S(2)}) async-start(), calls=%async_computation.14 | async-start | bytes 196608 | tf_op jit(solution)/shard_map/reduce_scatter | solution.py:196
  193.9 133.5 %reduce-scatter.17.cloned.1.call-start = ((), (), s32[]{:S(2)}) async-start(), calls=%async_computation.17 | async-start | bytes 196608 | tf_op jit(solution)/shard_map/reduce_scatter | solution.py:197
  232.3 122.3 %all-gather.6.cloned.1.call-start = ((), (), s32[]{:S(2)}) async-start(), calls=%async_computation.11 | async-start | bytes 12582912 | tf_op jit(solution)/shard_map/all_gather | solution.py:112
  362.8 22.2 %all-to-all-start.1 = ((bf16[4,64,512]{2,1,0:T(8,128)(2,1)}), bf16[4,64,512]{2,1,0:T(8,128)(2,1)}, u32[]{:S(2)}, u32[]{:S(2)}) async-start(bf16[4,64,512]{2,1,0:T(8,128)(2,1)} %copy.69), calls=%async_computation.1 | async-start | bytes 524288 | tf_op jit(solution)/shard_map/all_to_all | solution.py:131
  380.4 6.7 %copy-start.3 = (bf16[16,8,32,128]{3,2,1,0:T(8,128)(2,1)S(1)}, bf16[16,8,32,128]{3,2,1,0:T(8,128)(2,1)}, u32[]{:S(2)}) copy-start(bf16[16,8,32,128]{3,2,1,0:T(8,128)(2,1)} %copy-done.2) | copy-start | bytes 3145732
  386.4 0.7 copy-start.8
  389.3 2.9 copy-start.7
  394.4 11.3 %all-to-all-start.3 = ((bf16[4,64,512]{2,1,0:T(8,128)(2,1)}), bf16[4,64,512]{2,1,0:T(8,128)(2,1)S(1)}, u32[]{:S(2)}, u32[]{:S(2)}) async-start(bf16[4,64,512]{2,1,0:T(8,128)(2,1)} %copy.83), calls=%async_computation.3 | async-start | bytes 524288 | tf_op jit(solution)/shard_map/all_to_all | solution.py:158
  399.7 7.8 %copy-start.1 = (bf16[1,128,512]{2,1,0:T(8,128)(2,1)S(1)}, bf16[1,128,512]{2,1,0:T(8,128)(2,1)}, u32[]{:S(2)}) copy-start(bf16[1,128,512]{2,1,0:T(8,128)(2,1)} %param.14) | copy-start | bytes 393220
  400.4 6.4 %copy-start.9 = (bf16[128,512]{1,0:T(8,128)(2,1)S(1)}, bf16[128,512]{1,0:T(8,128)(2,1)}, u32[]{:S(2)}) copy-start(bf16[128,512]{1,0:T(8,128)(2,1)} %all_gather.27) | copy-start | bytes 393220
Sparse Core Ops, SparseCore 0:
  64.3 54.6 reduce-scatter.6
  121.6 48.0 reduce-scatter.12
  172.2 21.6 reduce-scatter.8
  196.3 35.9 reduce-scatter.14
  233.9 58.2 all-gather.3
  294.5 13.9 reduce-scatter.10
  310.9 16.4 reduce-scatter.16
  329.2 25.3 all-gather.5
